TPU v7x, 32 devices: a whole 2x2x4 slice. The times are simulated.
32 devices in a mesh: tok: 4 (over y, x), voc: 8 (over z, core).
Axes of the slice: x: 2, y: 2, z: 4, core: 2. Of those that a mesh axis runs over, the one named last changes fastest.
Arguments:
- hidden: bfloat16 [8192, 2048], P(('tok', 'voc')), as said below
- gain: bfloat16 [2048], replicated, may hold values from 0.5 to 1.5
- head: bfloat16 [2048, 50304], P(None, 'voc')
- targets: int32 [8192], replicated, may hold values from 0 to 50303
- lengths: int32 [8], replicated, may hold values from 1 to 1024, 5120 in all
- perm: int32 [8], replicated, may hold values from 0 to 7, each once
Outputs:
- logprob: float32 [5120], P(('tok', 'voc'))
- entropy: float32 [5120], P(('tok', 'voc'))
Inputs may be any that keep to these rules, and one draw needn't show every extreme that they name: Each request has at least one token and the longest has exactly 1024; the lengths sum to 5120. `perm`: each request is held by exactly one slot. `hidden`: rows past a request's length in its slot are not read by any output.
All inputs are finite; a program needn't handle non-finite values.
Results may differ from a plain program's by a relative error of at most 0.0024.
Values may be sent and summed in bfloat16 or wider, within the bound.
No kernel may reach another device: no remote copies, remote signals or barrier semaphores. Data moves between devices by JAX's collectives and lax.ppermute only.
A program may use at most 256 MiB of HBM per device.

v0:
```python
import jax
import jax.numpy as jnp
from jax import lax
from jax.sharding import PartitionSpec as P

MAXLEN = 1024


def slot_rows(positions, lengths, perm):
    count = lengths.shape[0]
    ident = jnp.arange(count, dtype=jnp.int32)
    starts = jnp.cumsum(lengths) - lengths
    request = jnp.sum((positions[:, None] >= starts[None, :]).astype(jnp.int32), axis=1) - 1
    start_of = jnp.sum(jnp.where(ident[None, :] == request[:, None], starts[None, :], 0), axis=1)
    slot_of = jnp.sum(jnp.where(perm[None, :] == request[:, None], ident[None, :], 0), axis=1)
    return slot_of * MAXLEN + positions - start_of


def row_stats(piece, weights, wanted):
    logits = jnp.dot(piece, weights, preferred_element_type=jnp.float32)
    top = jnp.max(logits, axis=1)
    expo = jnp.exp(logits - top[:, None])
    total = jnp.sum(expo, axis=1)
    moment = jnp.sum(expo * logits, axis=1)
    columns = jnp.arange(logits.shape[1], dtype=jnp.int32)
    picked = jnp.sum(jnp.where(columns[None, :] == wanted[:, None], logits, 0.0), axis=1)
    return jnp.stack([top, total, moment, picked], axis=0)


def make_stats(weights, col_base, row_base, targets, slot_len):
    count = slot_len.shape[0]
    ident = jnp.arange(count, dtype=jnp.int32)

    def compute(piece, start):
        size = piece.shape[0]
        rows = row_base + jnp.arange(size, dtype=jnp.int32)
        slot = rows // MAXLEN
        row_len = jnp.sum(jnp.where(slot[:, None] == ident[None, :], slot_len[None, :], 0), axis=1)
        live = rows % MAXLEN < row_len
        wanted = lax.dynamic_slice_in_dim(targets, row_base, size, 0) - col_base

        def busy(operand):
            return row_stats(piece, weights, wanted)

        def quiet(operand):
            zeros = jnp.zeros((size,), jnp.float32)
            return jnp.stack([zeros, zeros + 1.0, zeros, zeros], axis=0)

        return lax.cond(jnp.any(live), busy, quiet, 0)

    return compute


def finish(top, total, moment, picked):
    lse = top + jnp.log(total)
    return (picked - lse, lse - moment / total)


def on_device(hidden, gain, head, targets, lengths, perm):
    values = hidden.astype(jnp.float32)
    scale = lax.rsqrt(jnp.mean(values * values, axis=1, keepdims=True) + 1e-06)
    normed = (values * scale * gain.astype(jnp.float32)[None, :]).astype(jnp.bfloat16)
    count = lengths.shape[0]
    ident = jnp.arange(count, dtype=jnp.int32)
    slot_len = jnp.sum(jnp.where(perm[:, None] == ident[None, :], lengths[None, :], 0), axis=1)
    n_tok = lax.axis_size("tok")
    n_voc = lax.axis_size("voc")
    shard_cols = head.shape[1]
    voc_index = lax.axis_index("voc")
    tok_index = lax.axis_index("tok")
    out_rows = count * MAXLEN * 5 // 8 // (n_tok * n_voc)
    device = lax.axis_index(("tok", "voc"))
    group_rows = normed.shape[0] * n_voc
    compute = make_stats(head, voc_index * shard_cols, tok_index * group_rows, targets, slot_len)
    stats = compute(lax.all_gather(normed, "voc", axis=0, tiled=True), jnp.int32(0))
    top = lax.pmax(stats[0], "voc")
    factor = jnp.exp(stats[0] - top)
    total, moment, picked = lax.psum((stats[1] * factor, stats[2] * factor, stats[3]), "voc")
    own_lp, own_ent = finish(top, total, moment, picked)
    row_logprob, row_entropy = (
        lax.all_gather(own_lp, "tok", axis=0, tiled=True),
        lax.all_gather(own_ent, "tok", axis=0, tiled=True),
    )
    positions = device * out_rows + jnp.arange(out_rows, dtype=jnp.int32)
    rows = slot_rows(positions, lengths, perm)
    return (row_logprob[rows], row_entropy[rows])


def solution(mesh):
    in_specs = (P(("tok", "voc"), None), P(), P(None, "voc"), P(), P(), P())
    out_specs = (P(("tok", "voc")), P(("tok", "voc")))
    return jax.shard_map(
        on_device, mesh=mesh, in_specs=in_specs, out_specs=out_specs, check_vma=False
    )
```

profile of v0, /device:TPU:0, one launch (start us, length us, event | category | flops | bytes accessed | tf_op | source)
XLA Modules:
  0.0 252.4 jit_solution(14086592134587553559)
XLA Ops:
  7.2 0.0 all-gather.2.cloned.1.call-start
  7.2 0.7 convert_element_type.17
  7.9 1.5 fusion.1
  9.4 2.5 %fusion.3 = bf16[256,2048]{1,0:T(8,128)(2,1)} fusion(bf16[256,2048]{1,0:T(8,128)(2,1)} %param.8, f32[2048]{0:T(1024)S(1)} %convert_element_type.17, f32[256]{0:T(256)S(1)} %add_rsqrt_fusion), kind=kLoop, calls=%fused_computation.13 | loop fusion | flops 2097152 | bytes 2106368 | tf_op jit(solution)/shard_map/convert_element_type | solution.py:62
  11.9 0.0 all-gather.2.cloned.1.call-update
  12.0 0.9 select_reduce_fusion.4
  12.9 0.1 select_reduce_fusion.1
  12.9 0.6 fusion.10
  14.2 0.8 reduce-window.9
  15.1 0.7 bitcast_subtract_fusion
  15.7 0.1 convert_reduce_fusion
  15.8 0.7 select_reduce_fusion.3
  16.6 80.3 %all-gather.2.cloned.1.call-done = bf16[2048,2048]{1,0:T(8,128)(2,1)} async-done(((bf16[256,2048]{1,0:T(8,128)(2,1)}), bf16[2048,2048]{1,0:T(8,128)(2,1)}) %all-gather.2.cloned.1.call-update) | async-done | bytes 8388624 | tf_op jit(solution)/shard_map/all_gather | solution.py:75
  96.9 87.8 %conditional.1 = (f32[4,2048]{1,0:T(4,128)S(1)}) conditional(s32[]{:T(128)} %convert_element_type.15, () %tuple.17, (bf16[2048,2048]{1,0:T(8,128)(2,1)}, bf16[2048,6288]{0,1:T(8,128)(2,1)}, s32[]{:T(128)}, s32[8192]{0:T(1024)}, s32[]{:T(128)}) %tuple.18), branch_computations={%region_4.5_spmd, %region_5.10_spmd} | conditional | flops 52850606080 | bytes 137297984 | solution.py:49
  96.9 0.8 dynamic-slice_subtract_fusion
  97.7 63.0 %fusion.14 = (f32[2048]{0:T(1024)S(1)}, f32[2048,6288]{0,1:T(8,128)}) fusion(bf16[2048,2048]{1,0:T(8,128)(2,1)} %get-tuple-element.43, bf16[2048,6288]{0,1:T(8,128)(2,1)} %get-tuple-element.70), kind=kOutput, calls=%fused_computation.49 | convolution fusion | flops 52760444928 | bytes 85663744 | tf_op jit(solution)/shard_map/cond/branch_1_fun/dot_general | solution.py:20
  160.7 23.9 %fusion = (f32[2048]{0:T(1024)S(1)}, f32[2048]{0:T(1024)S(1)}, f32[2048]{0:T(1024)S(1)}) fusion(f32[2048,6288]{0,1:T(8,128)} %get-tuple-element.83, f32[2048]{0:T(1024)S(1)} %get-tuple-element.82, s32[2048]{0:T(1024)S(1)} %dynamic-slice_subtract_fusion), kind=kLoop, calls=%fused_computation.6 | loop fusion | flops 90138624 | bytes 51552256 | tf_op jit(solution)/shard_map/cond/branch_1_fun/reduce_sum | solution.py:23
  184.7 14.3 %pmax.7 = f32[2048]{0:T(1024)S(1)} all-reduce(f32[2048]{0:T(1024)S(1)} %bitcast.16), channel_id=1, replica_groups=mesh['tok'=4,'voc'=8] {'voc'}, use_global_device_ids=true, to_apply=%region_11.12 | all-reduce | flops 2048 | bytes 16384 | tf_op jit(solution)/shard_map/pmax | solution.py:76
  199.0 26.0 %all-reduce = (f32[2048]{0:T(1024)S(1)}, f32[2048]{0:T(1024)S(1)}, f32[2048]{0:T(1024)S(1)}) all-reduce(f32[2048]{0:T(1024)S(1)} %bitcast.22, f32[2048]{0:T(1024)S(1)} %get-tuple-element.91, f32[2048]{0:T(1024)S(1)} %get-tuple-element.90), channel_id=1, replica_groups=mesh['tok'=4,'voc'=8] {'voc'}, use_global_device_ids=true, to_apply=%region_10.11 | all-reduce | flops 6144 | bytes 49152 | tf_op jit(solution)/shard_map/psum | solution.py:78
  225.0 8.3 %all_gather.11 = f32[8192]{0:T(1024)S(1)} all-gather(f32[2048]{0:T(1024)S(1)} %get-tuple-element.88), channel_id=1, replica_groups=mesh['tok'=4,'voc'=8] {'tok'}, dimensions={0}, use_global_device_ids=true | all-gather | bytes 40960 | tf_op jit(solution)/shard_map/all_gather | solution.py:82
  233.3 8.1 %all_gather.10 = f32[8192]{0:T(1024)S(1)} all-gather(f32[2048]{0:T(1024)S(1)} %get-tuple-element.89), channel_id=1, replica_groups=mesh['tok'=4,'voc'=8] {'tok'}, dimensions={0}, use_global_device_ids=true | all-gather | bytes 40960 | tf_op jit(solution)/shard_map/all_gather | solution.py:81
  241.5 2.0 gather_fusion.1
  243.5 2.0 gather_fusion
  (11 shorter events, 0.1 us)
Async XLA Ops:
  7.2 89.7 %all-gather.2.cloned.1.call-start = ((), (), s32[]{:S(2)}) async-start(), calls=%async_computation | async-start | bytes 9437184 | tf_op jit(solution)/shard_map/all_gather | solution.py:75
Sparse Core Ops, SparseCore 0:
  12.1 84.7 all-gather.1
where the time goes:
time: 253 us; the launch traced here: 252 us
  waiting for transfers between devices  80.3 us (32%)
  matrix products  63 us (25%)
  blocking collectives  56.7 us (22%)
  other arithmetic  33.5 us (13%)
  between operations  14.8 us (6%)
  local copies, waits for them, and re-layouts  4.07 us (2%)
    all_gather x1, waiting for transfers between devices, on_device(): lax.all_gather(normed, 'voc', axis=0, tiled=True)  80.3 us
    dot_general x1, matrix products, row_stats(): logits = jnp.dot(piece, weights, preferred_element_type=jnp.float32)  63 us
    psum x1, blocking collectives, on_device(): lax.psum((stats[1] * factor, stats[2] * factor, stats[3]), 'voc')  26 us
    reduce_sum x1, other arithmetic, row_stats(): total = jnp.sum(expo, axis=1)  23.9 us
    pmax x1, blocking collectives, on_device(): top = lax.pmax(stats[0], 'voc')  14.3 us
    all_gather x1, blocking collectives, on_device(): lax.all_gather(own_ent, 'tok', axis=0, tiled=True)  8.35 us
    all_gather x1, blocking collectives, on_device(): lax.all_gather(own_lp, 'tok', axis=0, tiled=True)  8.14 us
  transfers between devices with their start and end apart: 1, of which 1 were waited for; matrix products, arithmetic and copies ran while one was open for 2% of the time, Pallas kernels for 0%

commit v1 on v0

--- a/solution.py
+++ b/solution.py
@@ -4,6 +4,25 @@
 from jax.sharding import PartitionSpec as P
 
 MAXLEN = 1024
+
+
+def derive_outputs(original):
+    base_arr = lax.psum(1, "voc")
+    e_next = lax.axis_index("voc")
+    current_block, response, carry_out = (base_arr, e_next, original.shape[0])
+    ledger = [(j, (j + 1) % current_block) for j in range(current_block)]
+    after = jnp.zeros(
+        (*original.shape[:0], current_block * carry_out, *original.shape[1:]), original.dtype
+    )
+    carry_in = original
+    i = 0
+    while i < current_block:
+        now = (response - i) % current_block
+        after = lax.dynamic_update_slice_in_dim(after, carry_in, now * carry_out, axis=0)
+        if i < current_block - 1:
+            carry_in = lax.ppermute(carry_in, "voc", ledger)
+        i = i + 1
+    return after
 
 
 def slot_rows(positions, lengths, perm):
@@ -72,7 +91,7 @@
     device = lax.axis_index(("tok", "voc"))
     group_rows = normed.shape[0] * n_voc
     compute = make_stats(head, voc_index * shard_cols, tok_index * group_rows, targets, slot_len)
-    stats = compute(lax.all_gather(normed, "voc", axis=0, tiled=True), jnp.int32(0))
+    stats = compute(derive_outputs(normed), jnp.int32(0))
     top = lax.pmax(stats[0], "voc")
     factor = jnp.exp(stats[0] - top)
     total, moment, picked = lax.psum((stats[1] * factor, stats[2] * factor, stats[3]), "voc")

time: 253 us -> 289 us (1.14)
  waiting for transfers between devices: 80.3 us -> 109 us
  local copies, waits for them, and re-layouts: 4.07 us -> 25.2 us
  between operations: 14.8 us -> 1.37 us
    ppermute x0 -> x7, waiting for transfers between devices: none -> 109 us  [derive_outputs(): carry_in = lax.ppermute(carry_in, 'voc', ledger)]
    all_gather x1 -> x0, waiting for transfers between devices: 80.3 us -> none  [on_device(): lax.all_gather(normed, 'voc', axis=0, tiled=True)]
    dynamic_update_slice x0 -> x8, local copies, waits for them, and re-layouts: none -> 14.8 us  [derive_outputs(): lax.dynamic_update_slice_in_dim(after, carry_in, now * carry_out, axis=0)]
    broadcast_in_dim x0 -> x1, local copies, waits for them, and re-layouts: none -> 4.33 us  [derive_outputs(): jnp.zeros((*original.shape[:0], current_block * carry_out, *original.shap...]
  transfers between devices with their start and end apart: 1 -> 7, of which waited for: 1 -> 7; matrix products, arithmetic and copies ran while one was open for 2% -> 1% of each run, Pallas kernels for 0% -> 0%
where the time goes in v1:
time: 289 us; the launch traced here: 288 us
  waiting for transfers between devices  109 us (38%)
  matrix products  63 us (22%)
  blocking collectives  56.8 us (20%)
  other arithmetic  32.5 us (11%)
  local copies, waits for them, and re-layouts  25.2 us (9%)
    ppermute x7, waiting for transfers between devices, derive_outputs(): carry_in = lax.ppermute(carry_in, 'voc', ledger)  109 us
    dot_general x1, matrix products, row_stats(): logits = jnp.dot(piece, weights, preferred_element_type=jnp.float32)  63 us
    psum x1, blocking collectives, on_device(): lax.psum((stats[1] * factor, stats[2] * factor, stats[3]), 'voc')  26 us
    reduce_sum x1, other arithmetic, row_stats(): total = jnp.sum(expo, axis=1)  23.9 us
    dynamic_update_slice x8, local copies, waits for them, and re-layouts, derive_outputs(): lax.dynamic_update_slice_in_dim(after, carry_in, now * carry_out, axis=0)  14.8 us
    pmax x1, blocking collectives, on_device(): top = lax.pmax(stats[0], 'voc')  13.9 us
    all_gather x1, blocking collectives, on_device(): lax.all_gather(own_ent, 'tok', axis=0, tiled=True)  8.7 us
    all_gather x1, blocking collectives, on_device(): lax.all_gather(own_lp, 'tok', axis=0, tiled=True)  8.14 us
  transfers between devices with their start and end apart: 7, of which 7 were waited for; matrix products, arithmetic and copies ran while one was open for 1% of the time, Pallas kernels for 0%

profile of v1, /device:TPU:0, one launch (start us, length us, event | category | flops | bytes accessed | tf_op | source)
XLA Modules:
  0.0 288.0 jit_solution(8080529540815183015)
XLA Ops:
  1.3 1.5 fusion.1
  2.8 1.5 fusion.3
  4.9 16.5 %collective-permute-done = bf16[256,2048]{1,0:T(8,128)(2,1)S(1)} collective-permute-done((bf16[256,2048]{1,0:T(8,128)(2,1)S(1)}, bf16[256,2048]{1,0:T(8,128)(2,1)S(1)}, u32[]{:S(2)}, u32[]{:S(2)}) %collective-permute-start) | collective-permute-done | bytes 1048608 | tf_op jit(solution)/shard_map/ppermute | solution.py:23
  21.4 16.0 %collective-permute-done.1 = bf16[256,2048]{1,0:T(8,128)(2,1)S(1)} collective-permute-done((bf16[256,2048]{1,0:T(8,128)(2,1)S(1)}, bf16[256,2048]{1,0:T(8,128)(2,1)S(1)}, u32[]{:S(2)}, u32[]{:S(2)}) %collective-permute-start.1) | collective-permute-done | bytes 1048608 | tf_op jit(solution)/shard_map/ppermute | solution.py:23
  37.5 16.0 %collective-permute-done.2 = bf16[256,2048]{1,0:T(8,128)(2,1)S(1)} collective-permute-done((bf16[256,2048]{1,0:T(8,128)(2,1)S(1)}, bf16[256,2048]{1,0:T(8,128)(2,1)S(1)}, u32[]{:S(2)}, u32[]{:S(2)}) %collective-permute-start.2) | collective-permute-done | bytes 1048608 | tf_op jit(solution)/shard_map/ppermute | solution.py:23
  54.5 16.0 %collective-permute-done.3 = bf16[256,2048]{1,0:T(8,128)(2,1)S(1)} collective-permute-done((bf16[256,2048]{1,0:T(8,128)(2,1)S(1)}, bf16[256,2048]{1,0:T(8,128)(2,1)S(1)}, u32[]{:S(2)}, u32[]{:S(2)}) %collective-permute-start.3) | collective-permute-done | bytes 1048608 | tf_op jit(solution)/shard_map/ppermute | solution.py:23
  71.5 16.1 %collective-permute-done.4 = bf16[256,2048]{1,0:T(8,128)(2,1)} collective-permute-done((bf16[256,2048]{1,0:T(8,128)(2,1)S(1)}, bf16[256,2048]{1,0:T(8,128)(2,1)}, u32[]{:S(2)}, u32[]{:S(2)}) %collective-permute-start.4) | collective-permute-done | bytes 1048608 | tf_op jit(solution)/shard_map/ppermute | solution.py:23
  90.7 13.2 %collective-permute-done.5 = bf16[256,2048]{1,0:T(8,128)(2,1)} collective-permute-done((bf16[256,2048]{1,0:T(8,128)(2,1)}, bf16[256,2048]{1,0:T(8,128)(2,1)}, u32[]{:S(2)}, u32[]{:S(2)}) %collective-permute-start.5) | collective-permute-done | bytes 1048608 | tf_op jit(solution)/shard_map/ppermute | solution.py:23
  105.5 14.8 %collective-permute-done.6 = bf16[256,2048]{1,0:T(8,128)(2,1)} collective-permute-done((bf16[256,2048]{1,0:T(8,128)(2,1)}, bf16[256,2048]{1,0:T(8,128)(2,1)}, u32[]{:S(2)}, u32[]{:S(2)}) %collective-permute-start.6) | collective-permute-done | bytes 1048608 | tf_op jit(solution)/shard_map/ppermute | solution.py:23
  120.3 106.9 %conditional.1 = (f32[4,2048]{1,0:T(4,128)S(1)}) conditional(s32[]{:T(128)} %convert_element_type.15, () %tuple.43, (pred[]{:T(512)}, bf16[256,2048]{1,0:T(8,128)(2,1)S(1)}, pred[]{:T(512)}, bf16[256,2048]{1,0:T(8,128)(2,1)S(1)}, pred[]{:T(512)}, /*index=5*/bf16[256,2048]{1,0:T(8,128)(2,1)S(1)}, pred[]{:T(512)}, ...), branch_computations={%region_4.5_spmd, %region_5.10_spmd.clone.clone} | conditional | flops 52850606080 | bytes 162464736 | solution.py:68
  120.3 4.3 %broadcast_in_dim.82 = bf16[2048,2048]{1,0:T(8,128)(2,1)} broadcast(bf16[]{:T(256)} %constant.129.clone.2), dimensions={} | broadcast | bytes 8388610 | tf_op jit(solution)/shard_map/broadcast_in_dim | solution.py:14
  127.8 2.3 constant_dynamic-update-slice_fusion.4
  130.2 2.3 constant_dynamic-update-slice_fusion.3
  132.4 2.3 constant_dynamic-update-slice_fusion.2
  134.7 2.4 constant_dynamic-update-slice_fusion.1
  137.1 2.3 constant_dynamic-update-slice_fusion
  139.4 63.0 %fusion.14 = (f32[2048]{0:T(1024)S(1)}, f32[2048,6288]{0,1:T(8,128)}) fusion(bf16[2048,2048]{1,0:T(8,128)(2,1)} %constant_dynamic-update-slice_fusion, bf16[2048,6288]{0,1:T(8,128)(2,1)} %get-tuple-element.715), kind=kOutput, calls=%fused_computation.57 | convolution fusion | flops 52760444928 | bytes 85663744 | tf_op jit(solution)/shard_map/cond/branch_1_fun/dot_general | solution.py:39
  203.2 23.9 %fusion = (f32[2048]{0:T(1024)S(1)}, f32[2048]{0:T(1024)S(1)}, f32[2048]{0:T(1024)S(1)}) fusion(f32[2048,6288]{0,1:T(8,128)} %get-tuple-element.792, f32[2048]{0:T(1024)S(1)} %get-tuple-element.791, s32[2048]{0:T(1024)S(1)} %dynamic-slice_subtract_fusion), kind=kLoop, calls=%fused_computation.6 | loop fusion | flops 90138624 | bytes 51552256 | tf_op jit(solution)/shard_map/cond/branch_1_fun/reduce_sum | solution.py:42
  227.2 13.9 %pmax.7 = f32[2048]{0:T(1024)S(1)} all-reduce(f32[2048]{0:T(1024)S(1)} %bitcast.20), channel_id=1, replica_groups=mesh['tok'=4,'voc'=8] {'voc'}, use_global_device_ids=true, to_apply=%region_11.12 | all-reduce | flops 2048 | bytes 16384 | tf_op jit(solution)/shard_map/pmax | solution.py:95
  241.2 26.0 %all-reduce = (f32[2048]{0:T(1024)S(1)}, f32[2048]{0:T(1024)S(1)}, f32[2048]{0:T(1024)S(1)}) all-reduce(f32[2048]{0:T(1024)S(1)} %bitcast.26, f32[2048]{0:T(1024)S(1)} %get-tuple-element.800, f32[2048]{0:T(1024)S(1)} %get-tuple-element.799), channel_id=1, replica_groups=mesh['tok'=4,'voc'=8] {'voc'}, use_global_device_ids=true, to_apply=%region_10.11 | all-reduce | flops 6144 | bytes 49152 | tf_op jit(solution)/shard_map/psum | solution.py:97
  267.1 8.7 %all_gather.7 = f32[8192]{0:T(1024)S(1)} all-gather(f32[2048]{0:T(1024)S(1)} %get-tuple-element.797), channel_id=1, replica_groups=mesh['tok'=4,'voc'=8] {'tok'}, dimensions={0}, use_global_device_ids=true | all-gather | bytes 40960 | tf_op jit(solution)/shard_map/all_gather | solution.py:101
  275.9 8.1 %all_gather.6 = f32[8192]{0:T(1024)S(1)} all-gather(f32[2048]{0:T(1024)S(1)} %get-tuple-element.798), channel_id=1, replica_groups=mesh['tok'=4,'voc'=8] {'tok'}, dimensions={0}, use_global_device_ids=true | all-gather | bytes 40960 | tf_op jit(solution)/shard_map/all_gather | solution.py:100
  284.0 2.0 gather_fusion.1
  286.0 2.0 gather_fusion
  (34 shorter events, 11.3 us)
Async XLA Ops:
  4.4 17.1 %collective-permute-start = (bf16[256,2048]{1,0:T(8,128)(2,1)S(1)}, bf16[256,2048]{1,0:T(8,128)(2,1)S(1)}, u32[]{:S(2)}, u32[]{:S(2)}) collective-permute-start(bf16[256,2048]{1,0:T(8,128)(2,1)S(1)} %fusion.3), channel_id=1, source_target_pairs={{0,1},{1,2},{2,3},{3,4},{4,5},{5,6},{6,7},{7,0},{8,9},{9,10},{10,1... | collective-permute-start | bytes 3145736 | tf_op jit(solution)/shard_map/ppermute | solution.py:23
  21.4 16.0 %collective-permute-start.1 = (bf16[256,2048]{1,0:T(8,128)(2,1)S(1)}, bf16[256,2048]{1,0:T(8,128)(2,1)S(1)}, u32[]{:S(2)}, u32[]{:S(2)}) collective-permute-start(bf16[256,2048]{1,0:T(8,128)(2,1)S(1)} %collective-permute-done), channel_id=1, source_target_pairs={{0,1},{1,2},{2,3},{3,4},{4,5},{5,6},{6,7},{7,0},{8,9},{9,10},{10,1... | collective-permute-start | bytes 3145736 | tf_op jit(solution)/shard_map/ppermute | solution.py:23
  37.5 16.0 %collective-permute-start.2 = (bf16[256,2048]{1,0:T(8,128)(2,1)S(1)}, bf16[256,2048]{1,0:T(8,128)(2,1)S(1)}, u32[]{:S(2)}, u32[]{:S(2)}) collective-permute-start(bf16[256,2048]{1,0:T(8,128)(2,1)S(1)} %collective-permute-done.1), channel_id=1, source_target_pairs={{0,1},{1,2},{2,3},{3,4},{4,5},{5,6},{6,7},{7,0},{8,9},{9,10},{10,1... | collective-permute-start | bytes 3145736 | tf_op jit(solution)/shard_map/ppermute | solution.py:23
  53.5 1.0 copy-start
  54.5 16.0 %collective-permute-start.3 = (bf16[256,2048]{1,0:T(8,128)(2,1)S(1)}, bf16[256,2048]{1,0:T(8,128)(2,1)S(1)}, u32[]{:S(2)}, u32[]{:S(2)}) collective-permute-start(bf16[256,2048]{1,0:T(8,128)(2,1)S(1)} %collective-permute-done.2), channel_id=1, source_target_pairs={{0,1},{1,2},{2,3},{3,4},{4,5},{5,6},{6,7},{7,0},{8,9},{9,10},{10,1... | collective-permute-start | bytes 3145736 | tf_op jit(solution)/shard_map/ppermute | solution.py:23
  70.5 1.0 copy-start.1
  71.5 16.1 %collective-permute-start.4 = (bf16[256,2048]{1,0:T(8,128)(2,1)S(1)}, bf16[256,2048]{1,0:T(8,128)(2,1)}, u32[]{:S(2)}, u32[]{:S(2)}) collective-permute-start(bf16[256,2048]{1,0:T(8,128)(2,1)S(1)} %collective-permute-done.3), channel_id=1, source_target_pairs={{0,1},{1,2},{2,3},{3,4},{4,5},{5,6},{6,7},{7,0},{8,9},{9,10},{10,1... | collective-permute-start | bytes 3145736 | tf_op jit(solution)/shard_map/ppermute | solution.py:23
  87.6 16.3 %collective-permute-start.5 = (bf16[256,2048]{1,0:T(8,128)(2,1)}, bf16[256,2048]{1,0:T(8,128)(2,1)}, u32[]{:S(2)}, u32[]{:S(2)}) collective-permute-start(bf16[256,2048]{1,0:T(8,128)(2,1)} %collective-permute-done.4), channel_id=1, source_target_pairs={{0,1},{1,2},{2,3},{3,4},{4,5},{5,6},{6,7},{7,0},{8,9},{9,10},{10,1... | collective-permute-start | bytes 3145736 | tf_op jit(solution)/shard_map/ppermute | solution.py:23
  104.0 16.3 %collective-permute-start.6 = (bf16[256,2048]{1,0:T(8,128)(2,1)}, bf16[256,2048]{1,0:T(8,128)(2,1)}, u32[]{:S(2)}, u32[]{:S(2)}) collective-permute-start(bf16[256,2048]{1,0:T(8,128)(2,1)} %collective-permute-done.5), channel_id=1, source_target_pairs={{0,1},{1,2},{2,3},{3,4},{4,5},{5,6},{6,7},{7,0},{8,9},{9,10},{10,1... | collective-permute-start | bytes 3145736 | tf_op jit(solution)/shard_map/ppermute | solution.py:23
